TPU v7x, 32 devices: a whole 2x2x4 slice. The times are simulated.
32 devices in a mesh: dp: 8 (over y, x, core), fsdp: 4 (over z).
Axes of the slice: x: 2, y: 2, z: 4, core: 2. Of those that a mesh axis runs over, the one named last changes fastest.
Arguments:
- tokens: bfloat16 [64, 256, 768], P(('dp', 'fsdp')), may hold values from -6 to 6
- band_waves: int32 [64, 13], P(('dp', 'fsdp')), may hold values from 0 to 128, as said below
- visible_slot: int32 [64, 256], P(('dp', 'fsdp')), may hold values from 0 to 1023, as said below
- wave_table: bfloat16 [128, 768], P(('dp', 'fsdp')), may hold values from -1.75 to 1.75
- norm1_gain: bfloat16 [768], P(('dp', 'fsdp')), may hold values from 0.5 to 1.5
- norm1_bias: bfloat16 [768], P(('dp', 'fsdp')), may hold values from -1.75 to 1.75
- qkv_weight: bfloat16 [768, 2304], P(('dp', 'fsdp')), may hold values from -0.3125 to 0.3125
- out_weight: bfloat16 [768, 768], P(('dp', 'fsdp')), may hold values from -0.875 to 0.875
- norm2_gain: bfloat16 [768], P(('dp', 'fsdp')), may hold values from 0.5 to 1.5
- norm2_bias: bfloat16 [768], P(('dp', 'fsdp')), may hold values from -1.75 to 1.75
- mlp_in: bfloat16 [768, 3072], P(('dp', 'fsdp')), may hold values from -0.21875 to 0.21875
- mlp_in_bias: bfloat16 [3072], P(('dp', 'fsdp')), may hold values from -3 to 3
- mlp_out: bfloat16 [3072, 768], P(('dp', 'fsdp')), may hold values from -0.15625 to 0.15625
- mlp_out_bias: bfloat16 [768], P(('dp', 'fsdp')), may hold values from -1.75 to 1.75
- dec_weight: bfloat16 [768, 512], P(('dp', 'fsdp')), may hold values from -0.21875 to 0.21875
- dec_bias: bfloat16 [512], P(('dp', 'fsdp')), may hold values from -1.75 to 1.75
- mask_token: bfloat16 [512], P(('dp', 'fsdp')), may hold values from -6 to 6
- cot_decoded: bfloat16 [64, 1024, 512], P(None, ('dp', 'fsdp')), may hold values from -6 to 6
Outputs:
- decoded: bfloat16 [64, 1024, 512], P(None, ('dp', 'fsdp'))
- grad_tokens: float32 [64, 256, 768], P(('dp', 'fsdp'))
- grad_wave_table: float32 [128, 768], P(('dp', 'fsdp'))
- grad_norm1_gain: float32 [768], P(('dp', 'fsdp'))
- grad_norm1_bias: float32 [768], P(('dp', 'fsdp'))
- grad_qkv_weight: float32 [768, 2304], P(('dp', 'fsdp'))
- grad_out_weight: float32 [768, 768], P(('dp', 'fsdp'))
- grad_norm2_gain: float32 [768], P(('dp', 'fsdp'))
- grad_norm2_bias: float32 [768], P(('dp', 'fsdp'))
- grad_mlp_in: float32 [768, 3072], P(('dp', 'fsdp'))
- grad_mlp_in_bias: float32 [3072], P(('dp', 'fsdp'))
- grad_mlp_out: float32 [3072, 768], P(('dp', 'fsdp'))
- grad_mlp_out_bias: float32 [768], P(('dp', 'fsdp'))
- grad_dec_weight: float32 [768, 512], P(('dp', 'fsdp'))
- grad_dec_bias: float32 [512], P(('dp', 'fsdp'))
- grad_mask_token: float32 [512], P(('dp', 'fsdp'))
Inputs may be any that keep to these rules, and one draw needn't show every extreme that they name: `band_waves`: the first 4 entries of a row are ids below 128; an entry equal to 128 marks an unused band slot, so a chip has 4 to 13 bands; ids may repeat. `visible_slot`: the 256 entries of a row are distinct; the other slots of that chip hold the mask token.
All inputs are finite; a program needn't handle non-finite values.
Results may differ from a plain program's by a relative error of at most 0.012.
The roundings to bfloat16 on the way count: a program that leaves them out, or rounds other values in their place, can miss the bound.
Values may be sent and summed in bfloat16 or wider, within the bound.
No kernel may reach another device: no remote copies, remote signals or barrier semaphores. Data moves between devices by JAX's collectives and lax.ppermute only.
A program may use at most 128 MiB of HBM per device.

v0:
```python
import jax
import jax.numpy as jnp
from jax import lax
from jax.sharding import PartitionSpec as P

D = 768
HD = 64
DEC = 512
WAVES = 128
L = 1024
NORM_EPSILON = 1e-05
ROOT_HALF = 0.7071067811865476
INVERSE_ROOT_TAU = 0.3989422804014327
HIGH_PRECISION = lax.Precision.HIGHEST


def product(left_op, right_op):
    return jnp.dot(left_op, right_op, preferred_element_type=jnp.float32)


def inner_rows(left_op, right_op):
    return lax.dot_general(
        left_op, right_op, (((0,), (0,)), ((), ())), preferred_element_type=jnp.float32
    )


def outer_cols(left_op, right_op):
    return lax.dot_general(
        left_op, right_op, (((1,), (1,)), ((), ())), preferred_element_type=jnp.float32
    )


def norm_forward(residual, gain, shift):
    mean_val = jnp.mean(residual, axis=-1, keepdims=True)
    centered = residual - mean_val
    variance = jnp.mean(centered * centered, axis=-1, keepdims=True)
    inverse = lax.rsqrt(variance + NORM_EPSILON)
    normed = centered * inverse
    return (normed * gain + shift, normed, inverse)


def norm_backward(incoming, normed, inverse, gain):
    scaled = incoming * gain
    first_mean = jnp.mean(scaled, axis=-1, keepdims=True)
    second_mean = jnp.mean(scaled * normed, axis=-1, keepdims=True)
    grad_input = inverse * (scaled - first_mean - normed * second_mean)
    return (grad_input, jnp.sum(incoming * normed, axis=0), jnp.sum(incoming, axis=0))


def gelu_value(hidden):
    return 0.5 * hidden * (1.0 + lax.erf(hidden * ROOT_HALF))


def gelu_slope(hidden):
    return (
        0.5 * (1.0 + lax.erf(hidden * ROOT_HALF))
        + hidden * jnp.exp(-0.5 * hidden * hidden) * INVERSE_ROOT_TAU
    )


def head_slice(source, pair_index):
    chip_count, vis_len, feature_width = source.shape
    piece = lax.dynamic_slice_in_dim(source, pair_index * 2 * HD, 2 * HD, axis=2)
    return piece.reshape(chip_count, vis_len, 2, HD)


def attend(queries, key_rows, value_rows):
    chip_count, vis_len, feature_width = queries.shape
    score_scale = HD ** (-0.5)

    def one_pair(pair_index):
        query_part = head_slice(queries, pair_index)
        key_part = head_slice(key_rows, pair_index)
        value_part = head_slice(value_rows, pair_index)
        scores = (
            jnp.einsum("cqhd,ckhd->chqk", query_part, key_part, preferred_element_type=jnp.float32)
            * score_scale
        )
        row_peak = jnp.max(scores, axis=-1, keepdims=True)
        exponents = jnp.exp(scores - row_peak)
        row_total = jnp.sum(exponents, axis=-1, keepdims=True)
        soft_weights = (exponents / row_total).astype(jnp.bfloat16)
        mixture = jnp.einsum(
            "chqk,ckhd->cqhd", soft_weights, value_part, preferred_element_type=jnp.float32
        )
        return (
            mixture.astype(jnp.bfloat16).reshape(chip_count, vis_len, 2 * HD),
            row_peak + jnp.log(row_total),
        )

    mixtures, log_totals = lax.map(one_pair, jnp.arange(feature_width // (2 * HD)))
    merged = mixtures.transpose(1, 2, 0, 3).reshape(chip_count * vis_len, feature_width)
    return (merged, log_totals)


def attend_back(queries, key_rows, value_rows, log_totals, grad_mixture):
    chip_count, vis_len, feature_width = queries.shape
    score_scale = HD ** (-0.5)
    part_shape = (chip_count, vis_len, 2 * HD)

    def one_pair(inputs):
        pair_index, log_total = inputs
        query_part = head_slice(queries, pair_index)
        key_part = head_slice(key_rows, pair_index)
        value_part = head_slice(value_rows, pair_index)
        grad_part = head_slice(grad_mixture, pair_index)
        scores = (
            jnp.einsum("cqhd,ckhd->chqk", query_part, key_part, preferred_element_type=jnp.float32)
            * score_scale
        )
        soft_full = jnp.exp(scores - log_total)
        soft_low = soft_full.astype(jnp.bfloat16)
        grad_values = jnp.einsum(
            "chqk,cqhd->ckhd", soft_low, grad_part, preferred_element_type=jnp.float32
        )
        grad_soft = jnp.einsum(
            "cqhd,ckhd->chqk", grad_part, value_part, preferred_element_type=jnp.float32
        )
        row_delta = jnp.sum(grad_soft * soft_full, axis=-1, keepdims=True)
        grad_scores = (soft_full * (grad_soft - row_delta)).astype(jnp.bfloat16)
        grad_queries = (
            jnp.einsum("chqk,ckhd->cqhd", grad_scores, key_part, preferred_element_type=jnp.float32)
            * score_scale
        )
        grad_keys = (
            jnp.einsum(
                "chqk,cqhd->ckhd", grad_scores, query_part, preferred_element_type=jnp.float32
            )
            * score_scale
        )
        return (
            grad_queries.reshape(part_shape),
            grad_keys.reshape(part_shape),
            grad_values.reshape(part_shape),
        )

    grad_q_all, grad_k_all, grad_v_all = lax.map(
        one_pair, (jnp.arange(feature_width // (2 * HD)), log_totals)
    )
    flat_rows = chip_count * vis_len
    return (
        grad_q_all.transpose(1, 2, 0, 3).reshape(flat_rows, feature_width),
        grad_k_all.transpose(1, 2, 0, 3).reshape(flat_rows, feature_width),
        grad_v_all.transpose(1, 2, 0, 3).reshape(flat_rows, feature_width),
    )


def local(
    tokens,
    band_waves,
    visible_slot,
    wave_table,
    norm1_gain,
    norm1_bias,
    qkv_weight,
    out_weight,
    norm2_gain,
    norm2_bias,
    mlp_in,
    mlp_in_bias,
    mlp_out,
    mlp_out_bias,
    dec_weight,
    dec_bias,
    mask_token,
    cot_decoded,
):
    shards = (
        wave_table,
        norm1_gain,
        norm1_bias,
        qkv_weight,
        out_weight,
        norm2_gain,
        norm2_bias,
        mlp_in,
        mlp_in_bias,
        mlp_out,
        mlp_out_bias,
        dec_weight,
        dec_bias,
        mask_token,
    )
    gathered = (
        lax.all_gather(shards[0], ("dp", "fsdp"), axis=0, tiled=True),
        lax.all_gather(shards[1], ("dp", "fsdp"), axis=0, tiled=True),
        lax.all_gather(shards[2], ("dp", "fsdp"), axis=0, tiled=True),
        lax.all_gather(shards[3], ("dp", "fsdp"), axis=0, tiled=True),
        lax.all_gather(shards[4], ("dp", "fsdp"), axis=0, tiled=True),
        lax.all_gather(shards[5], ("dp", "fsdp"), axis=0, tiled=True),
        lax.all_gather(shards[6], ("dp", "fsdp"), axis=0, tiled=True),
        lax.all_gather(shards[7], ("dp", "fsdp"), axis=0, tiled=True),
        lax.all_gather(shards[8], ("dp", "fsdp"), axis=0, tiled=True),
        lax.all_gather(shards[9], ("dp", "fsdp"), axis=0, tiled=True),
        lax.all_gather(shards[10], ("dp", "fsdp"), axis=0, tiled=True),
        lax.all_gather(shards[11], ("dp", "fsdp"), axis=0, tiled=True),
        lax.all_gather(shards[12], ("dp", "fsdp"), axis=0, tiled=True),
        lax.all_gather(shards[13], ("dp", "fsdp"), axis=0, tiled=True),
    )
    (
        wave_full,
        gain_one,
        shift_one,
        qkv_full,
        out_full,
        gain_two,
        shift_two,
        inner_full,
        inner_bias,
        outer_full,
        outer_bias,
        dec_full,
        dec_shift,
        mask_full,
    ) = gathered
    chip_count, vis_len, feature_width = tokens.shape
    row_count = chip_count * vis_len
    counts = jnp.sum(
        (band_waves[:, :, None] == jnp.arange(WAVES, dtype=jnp.int32)[None, None, :]).astype(
            jnp.float32
        ),
        axis=1,
    )
    spectral = jnp.dot(counts.astype(jnp.bfloat16), wave_full, preferred_element_type=jnp.float32)
    residual = (tokens.astype(jnp.float32) + spectral[:, None, :]).reshape(row_count, D)
    norm_out_one, normed_one, inverse_one = norm_forward(
        residual, gain_one.astype(jnp.float32), shift_one.astype(jnp.float32)
    )
    act_one = norm_out_one.astype(jnp.bfloat16)
    qkv_vals = product(act_one, qkv_full).astype(jnp.bfloat16)
    queries = qkv_vals[:, :D].reshape(chip_count, vis_len, D)
    key_rows = qkv_vals[:, D : 2 * D].reshape(chip_count, vis_len, D)
    value_rows = qkv_vals[:, 2 * D :].reshape(chip_count, vis_len, D)
    mixture, log_totals = attend(queries, key_rows, value_rows)
    res_one = residual + product(mixture, out_full)
    norm_out_two, normed_two, inverse_two = norm_forward(
        res_one, gain_two.astype(jnp.float32), shift_two.astype(jnp.float32)
    )
    act_two = norm_out_two.astype(jnp.bfloat16)
    hidden = product(act_two, inner_full) + inner_bias.astype(jnp.float32)
    active = gelu_value(hidden).astype(jnp.bfloat16)
    res_two = res_one + (product(active, outer_full) + outer_bias.astype(jnp.float32))
    enc_low = res_two.astype(jnp.bfloat16)
    projected = (product(enc_low, dec_full) + dec_shift.astype(jnp.float32)).astype(jnp.bfloat16)
    chip_index = jnp.arange(chip_count, dtype=jnp.int32)[:, None]
    filled = jnp.broadcast_to(mask_full, (chip_count, L, DEC))
    filled = filled.at[chip_index, visible_slot].set(projected.reshape(chip_count, vis_len, DEC))
    decoded = lax.all_to_all(filled, ("dp", "fsdp"), split_axis=1, concat_axis=0, tiled=True)
    grad_full = lax.all_to_all(cot_decoded, ("dp", "fsdp"), split_axis=0, concat_axis=1, tiled=True)
    back_weights = (
        lax.all_gather(shards[0], ("dp", "fsdp"), axis=0, tiled=True),
        lax.all_gather(shards[1], ("dp", "fsdp"), axis=0, tiled=True),
        lax.all_gather(shards[2], ("dp", "fsdp"), axis=0, tiled=True),
        lax.all_gather(shards[3], ("dp", "fsdp"), axis=0, tiled=True),
        lax.all_gather(shards[4], ("dp", "fsdp"), axis=0, tiled=True),
        lax.all_gather(shards[5], ("dp", "fsdp"), axis=0, tiled=True),
        lax.all_gather(shards[6], ("dp", "fsdp"), axis=0, tiled=True),
        lax.all_gather(shards[7], ("dp", "fsdp"), axis=0, tiled=True),
        lax.all_gather(shards[8], ("dp", "fsdp"), axis=0, tiled=True),
        lax.all_gather(shards[9], ("dp", "fsdp"), axis=0, tiled=True),
        lax.all_gather(shards[10], ("dp", "fsdp"), axis=0, tiled=True),
        lax.all_gather(shards[11], ("dp", "fsdp"), axis=0, tiled=True),
        lax.all_gather(shards[12], ("dp", "fsdp"), axis=0, tiled=True),
        lax.all_gather(shards[13], ("dp", "fsdp"), axis=0, tiled=True),
    )
    (
        unused_wave,
        back_gain_one,
        unused_shift_one,
        back_qkv,
        back_out,
        back_gain_two,
        unused_shift_two,
        back_inner,
        unused_inner_bias,
        back_outer,
        unused_outer_bias,
        back_dec,
        unused_dec_shift,
        unused_mask,
    ) = back_weights
    grad_vis_low = jnp.take_along_axis(grad_full, visible_slot[:, :, None], axis=1).reshape(
        row_count, DEC
    )
    grad_vis = grad_vis_low.astype(jnp.float32)
    grad_mask_token = jnp.sum(grad_full.astype(jnp.float32), axis=(0, 1)) - jnp.sum(
        grad_vis, axis=0
    )
    grad_dec_bias = jnp.sum(grad_vis, axis=0)
    grad_dec_weight = inner_rows(enc_low, grad_vis_low)
    grad_res_two = outer_cols(grad_vis_low, back_dec)
    grad_ffo = grad_res_two.astype(jnp.bfloat16)
    grad_mlp_out_bias = jnp.sum(grad_ffo.astype(jnp.float32), axis=0)
    grad_mlp_out = inner_rows(active, grad_ffo)
    grad_hidden = (outer_cols(grad_ffo, back_outer) * gelu_slope(hidden)).astype(jnp.bfloat16)
    grad_mlp_in_bias = jnp.sum(grad_hidden.astype(jnp.float32), axis=0)
    grad_mlp_in = inner_rows(act_two, grad_hidden)
    grad_act_two = outer_cols(grad_hidden, back_inner)
    grad_norm_two, grad_norm2_gain, grad_norm2_bias = norm_backward(
        grad_act_two, normed_two, inverse_two, back_gain_two.astype(jnp.float32)
    )
    grad_res_one = grad_res_two + grad_norm_two
    grad_att = grad_res_one.astype(jnp.bfloat16)
    grad_out_weight = inner_rows(mixture, grad_att)
    grad_mixed = outer_cols(grad_att, back_out).astype(jnp.bfloat16).reshape(chip_count, vis_len, D)
    grad_queries, grad_keys, grad_values = attend_back(
        queries, key_rows, value_rows, log_totals, grad_mixed
    )
    grad_qkv = jnp.concatenate([grad_queries, grad_keys, grad_values], axis=1).astype(jnp.bfloat16)
    grad_qkv_weight = inner_rows(act_one, grad_qkv)
    grad_act_one = outer_cols(grad_qkv, back_qkv)
    grad_norm_one, grad_norm1_gain, grad_norm1_bias = norm_backward(
        grad_act_one, normed_one, inverse_one, back_gain_one.astype(jnp.float32)
    )
    grad_tokens = (grad_res_one + grad_norm_one).reshape(chip_count, vis_len, D)
    chip_sums = jnp.sum(grad_tokens, axis=1)
    grad_wave_table = lax.dot_general(
        counts, chip_sums, (((0,), (0,)), ((), ())), precision=HIGH_PRECISION
    )
    local_grads = (
        grad_wave_table,
        grad_norm1_gain,
        grad_norm1_bias,
        grad_qkv_weight,
        grad_out_weight,
        grad_norm2_gain,
        grad_norm2_bias,
        grad_mlp_in,
        grad_mlp_in_bias,
        grad_mlp_out,
        grad_mlp_out_bias,
        grad_dec_weight,
        grad_dec_bias,
        grad_mask_token,
    )
    summed = (
        lax.psum_scatter(local_grads[0], ("dp", "fsdp"), scatter_dimension=0, tiled=True),
        lax.psum_scatter(local_grads[1], ("dp", "fsdp"), scatter_dimension=0, tiled=True),
        lax.psum_scatter(local_grads[2], ("dp", "fsdp"), scatter_dimension=0, tiled=True),
        lax.psum_scatter(local_grads[3], ("dp", "fsdp"), scatter_dimension=0, tiled=True),
        lax.psum_scatter(local_grads[4], ("dp", "fsdp"), scatter_dimension=0, tiled=True),
        lax.psum_scatter(local_grads[5], ("dp", "fsdp"), scatter_dimension=0, tiled=True),
        lax.psum_scatter(local_grads[6], ("dp", "fsdp"), scatter_dimension=0, tiled=True),
        lax.psum_scatter(local_grads[7], ("dp", "fsdp"), scatter_dimension=0, tiled=True),
        lax.psum_scatter(local_grads[8], ("dp", "fsdp"), scatter_dimension=0, tiled=True),
        lax.psum_scatter(local_grads[9], ("dp", "fsdp"), scatter_dimension=0, tiled=True),
        lax.psum_scatter(local_grads[10], ("dp", "fsdp"), scatter_dimension=0, tiled=True),
        lax.psum_scatter(local_grads[11], ("dp", "fsdp"), scatter_dimension=0, tiled=True),
        lax.psum_scatter(local_grads[12], ("dp", "fsdp"), scatter_dimension=0, tiled=True),
        lax.psum_scatter(local_grads[13], ("dp", "fsdp"), scatter_dimension=0, tiled=True),
    )
    return (
        decoded,
        grad_tokens,
        summed[0],
        summed[1],
        summed[2],
        summed[3],
        summed[4],
        summed[5],
        summed[6],
        summed[7],
        summed[8],
        summed[9],
        summed[10],
        summed[11],
        summed[12],
        summed[13],
    )


def solution(mesh):
    placed = (
        P(("dp", "fsdp"), None, None),
        P(("dp", "fsdp"), None),
        P(("dp", "fsdp"), None),
        P(("dp", "fsdp"), None),
        P(("dp", "fsdp")),
        P(("dp", "fsdp")),
        P(("dp", "fsdp"), None),
        P(("dp", "fsdp"), None),
        P(("dp", "fsdp")),
        P(("dp", "fsdp")),
        P(("dp", "fsdp"), None),
        P(("dp", "fsdp")),
        P(("dp", "fsdp"), None),
        P(("dp", "fsdp")),
        P(("dp", "fsdp"), None),
        P(("dp", "fsdp")),
        P(("dp", "fsdp")),
        P(None, ("dp", "fsdp"), None),
    )
    return jax.shard_map(
        local,
        mesh=mesh,
        in_specs=placed,
        out_specs=(
            P(None, ("dp", "fsdp"), None),
            P(("dp", "fsdp"), None, None),
            P(("dp", "fsdp"), None),
            P(("dp", "fsdp")),
            P(("dp", "fsdp")),
            P(("dp", "fsdp"), None),
            P(("dp", "fsdp"), None),
            P(("dp", "fsdp")),
            P(("dp", "fsdp")),
            P(("dp", "fsdp"), None),
            P(("dp", "fsdp")),
            P(("dp", "fsdp"), None),
            P(("dp", "fsdp")),
            P(("dp", "fsdp"), None),
            P(("dp", "fsdp")),
            P(("dp", "fsdp")),
        ),
        check_vma=False,
    )
```

profile of v0, /device:TPU:0, one launch (start us, length us, event | category | flops | bytes accessed | tf_op | source)
XLA Modules:
  0.0 1167.7 jit_solution(14192374103499020075)
XLA Ops:
  9.5 7.5 all-to-all-start.1
  17.7 123.0 %all-gather = bf16[32,4,768]{2,1,0:T(4,128)(2,1)S(1)} all-gather(bf16[1,4,768]{2,1,0:T(4,128)(2,1)S(1)} %bitcast.243), channel_id=1, replica_groups=mesh['dp'=8,'fsdp'=4] {'dp','fsdp'}, dimensions={0}, use_global_device_ids=true | all-gather | bytes 202752 | tf_op jit(solution)/shard_map/all_gather | solution.py:185
  142.8 37.7 %all-reduce.18 = (bf16[512]{0:T(512)(128)(2,1)S(1)}, bf16[768]{0:T(1024)(128)(2,1)S(1)}, bf16[768]{0:T(1024)(128)(2,1)S(1)}, bf16[768]{0:T(1024)(128)(2,1)S(1)},...) all-reduce(bf16[512]{0:T(512)(128)(2,1)S(1)} %dynamic-update-slice,, ...), channel_id=1, replica_groups=mesh['dp'=8,'fsdp'=4] {'dp','fsdp'}, use_global_device_ids=true, to_apply=%add | all-reduce | flops 7936 | bytes 31744
  181.5 1.2 add_convert_fusion.2
  182.8 83.6 %all_gather.61 = bf16[768,512]{1,0:T(8,128)(2,1)} all-gather(bf16[24,512]{1,0:T(8,128)(2,1)S(1)} %copy-done.19), channel_id=1, replica_groups=mesh['dp'=8,'fsdp'=4] {'dp','fsdp'}, dimensions={0}, use_global_device_ids=true | all-gather | bytes 811008 | tf_op jit(solution)/shard_map/all_gather | solution.py:196
  266.4 3.2 copy.128
  269.5 9.9 gather_fusion
  279.5 1.9 fusion.18
  281.4 4.8 convolution_convert_fusion.1
  286.2 1.5 fusion.35
  287.7 2.3 copy.121
  290.0 2.3 copy.122
  292.3 2.3 copy.123
  294.6 28.2 %while.30 = (s32[]{:T(128)}, bf16[6,2,256,128]{2,3,1,0:T(8,128)(2,1)}, f32[6,2,2,256,1]{3,2,1,4,0:T(2,128)S(1)}, s32[6]{0:T(128)S(1)}, bf16[2,256,768]{1,2,0:T(8...) while((s32[]{:T(128)}, ...), condition=%wide.region_6.7_spmd, body=%wide.region_3.6_spmd.sunk | while | flops 69008384 | bytes 4751551 | solution.py:91
  295.9 0.9 constant_dynamic-slice_fusion.14
  296.8 1.0 constant_dynamic-slice_fusion.15
  301.5 1.0 constant_dynamic-slice_fusion.15
  305.3 0.9 constant_dynamic-slice_fusion.14
  306.2 1.0 constant_dynamic-slice_fusion.15
  310.0 0.9 constant_dynamic-slice_fusion.14
  310.9 1.0 constant_dynamic-slice_fusion.15
  314.7 0.9 constant_dynamic-slice_fusion.14
  315.6 1.0 constant_dynamic-slice_fusion.15
  319.4 0.9 constant_dynamic-slice_fusion.14
  320.3 1.0 constant_dynamic-slice_fusion.15
  322.9 1.9 copy.124
  324.8 1.1 copy.144
  325.9 2.4 fusion.36
  328.3 1.1 copy-done.2
  329.8 8.4 multiply_convert_fusion.1
  338.1 7.5 convert_reduce_fusion
  345.6 3.1 multiply_reduce_fusion.1
  350.0 1.7 convolution_convert_fusion.2
  351.7 49.0 %while.31 = (s32[]{:T(128)}, bf16[6,2,256,128]{2,3,1,0:T(8,128)(2,1)}, bf16[6,2,256,128]{2,3,1,0:T(8,128)(2,1)}, bf16[6,2,256,128]{2,3,1,0:T(8,128)(2,1)}, s32[6...) while((s32[]{:T(128)}, ...), condition=%wide.region_14.15_spmd, body=%wide.region_12.14_spmd.sunk | while | flops 170130432 | bytes 11292899 | solution.py:137
  353.9 0.9 constant_dynamic-slice_fusion.17
  356.3 0.9 constant_dynamic-slice_fusion.19
  362.1 0.9 constant_dynamic-slice_fusion.17
  370.2 0.9 constant_dynamic-slice_fusion.17
  400.7 1.9 copy.133
  406.0 1.7 copy-done.24
  407.7 2.5 multiply_reduce_fusion.2
  410.8 1.1 copy-done.9
  412.0 1.3 fusion.37
  413.6 6.0 add_convert_fusion
  420.5 1.8 fusion.17
  422.3 3.3 fusion.14
  425.7 1.1 copy-done.11
  426.8 6.6 fusion.38
  433.5 7.2 fusion.32
  441.0 1.1 copy-done.1
  442.1 8.2 fusion.26
  450.4 1.1 copy-done.13
  452.4 26.7 %scatter_fusion = bf16[2,1024,512]{2,1,0:T(8,128)(2,1)S(1)} fusion(bf16[2,1024,512]{2,1,0:T(8,128)(2,1)S(1)} %broadcast_in_dim.84, s32[512]{0:T(512)S(1)} %bitcast.201, bf16[512,512]{1,0:T(8,128)(2,1)S(1)} %fusion.12), kind=kCustom, calls=%fused_computation.1 | custom fusion | bytes 1576960 | tf_op jit(solution)/shard_map/scatter | solution.py:247
  479.1 3.5 copy.125
  482.6 2.9 all-to-all-start
  485.7 1.9 convert_reduce_fusion.1
  487.6 68.5 %all-reduce.17 = (f32[768]{0:T(1024)S(1)}, f32[768]{0:T(1024)S(1)}, f32[768]{0:T(1024)S(1)}, f32[768]{0:T(1024)S(1)}, f32[3072]{0:T(1024)S(1)}, /*index=5*/f32[768]{0:T(1024)S(1)}, f32[512]{0:T(512)S(1)}, f32[512]{0:T(512)S(1)}) all-reduce(f32[768]{0:T(1024)S(1)} %get-tuple-element.342, ...), channel_id=3, replica_groups=mesh['dp'=8,'fsdp'=4] {'dp','fsdp'}, use_global_device_ids=true, to_apply=%region_20.21.clone | all-reduce | flops 7936 | bytes 63488
  560.9 1.3 constant_dynamic-slice_fusion.7
  562.5 1.6 copy.127
  564.1 84.0 %reduce-scatter.14.cloned.1.call-done = f32[24,512]{1,0:T(8,128)} async-done(((f32[768,512]{1,0:T(8,128)}), f32[24,512]{1,0:T(8,128)}) %reduce-scatter.14.cloned.1.call-update) | async-done | bytes 49168 | tf_op jit(solution)/shard_map/reduce_scatter | solution.py:348
  648.1 104.6 %reduce-scatter.8.cloned.1.call-done = f32[24,768]{1,0:T(8,128)} async-done(((f32[768,768]{1,0:T(8,128)}), f32[24,768]{1,0:T(8,128)}) %reduce-scatter.8.cloned.1.call-update) | async-done | bytes 73744 | tf_op jit(solution)/shard_map/reduce_scatter | solution.py:341
  752.6 124.8 %reduce-scatter.6.cloned.1.call-done = f32[24,2304]{1,0:T(8,128)} async-done(((f32[768,2304]{1,0:T(8,128)}), f32[24,2304]{1,0:T(8,128)}) %reduce-scatter.6.cloned.1.call-update) | async-done | bytes 221200 | tf_op jit(solution)/shard_map/reduce_scatter | solution.py:340
  877.5 141.6 %reduce-scatter.10.cloned.1.call-done = f32[24,3072]{1,0:T(8,128)} async-done(((f32[768,3072]{1,0:T(8,128)}), f32[24,3072]{1,0:T(8,128)}) %reduce-scatter.10.cloned.1.call-update) | async-done | bytes 294928 | tf_op jit(solution)/shard_map/reduce_scatter | solution.py:344
  1019.1 141.5 %reduce-scatter.12.cloned.1.call-done = f32[96,768]{1,0:T(8,128)} async-done(((f32[3072,768]{1,0:T(8,128)}), f32[96,768]{1,0:T(8,128)}) %reduce-scatter.12.cloned.1.call-update) | async-done | bytes 294928 | tf_op jit(solution)/shard_map/reduce_scatter | solution.py:346
  (287 shorter events, 73.7 us)
Async XLA Ops:
  7.2 274.2 %all-gather.6.cloned.1.call-start = ((), (), s32[]{:S(2)}) async-start(), calls=%async_computation.7 | async-start | bytes 3649536 | tf_op jit(solution)/shard_map/all_gather | solution.py:188
  7.9 317.9 %all-gather.8.cloned.1.call-start = ((), (), s32[]{:S(2)}) async-start(), calls=%async_computation.8 | async-start | bytes 1216512 | tf_op jit(solution)/shard_map/all_gather | solution.py:189
  8.7 321.1 %all-gather.10.cloned.1.call-start = ((), (), s32[]{:S(2)}) async-start(), calls=%async_computation.9 | async-start | bytes 4866048 | tf_op jit(solution)/shard_map/all_gather | solution.py:192
  9.4 8.3 copy-start.21
  9.4 131.4 %copy-start.22 = (s32[2,13]{1,0:T(2,128)S(1)}, s32[2,13]{1,0:T(2,128)}, u32[]{:S(2)}) copy-start(s32[2,13]{1,0:T(2,128)} %param.23) | copy-start | bytes 316
  9.4 131.5 %copy-start.25 = (bf16[24]{0:T(256)(128)(2,1)S(1)}, bf16[24]{0:T(256)(128)(2,1)}, u32[]{:S(2)}) copy-start(bf16[24]{0:T(256)(128)(2,1)} %param.27) | copy-start | bytes 148
  9.4 131.7 %copy-start.26 = (bf16[24]{0:T(256)(128)(2,1)S(1)}, bf16[24]{0:T(256)(128)(2,1)}, u32[]{:S(2)}) copy-start(bf16[24]{0:T(256)(128)(2,1)} %param.26) | copy-start | bytes 148
  9.4 131.9 %copy-start.27 = (bf16[24]{0:T(256)(128)(2,1)S(1)}, bf16[24]{0:T(256)(128)(2,1)}, u32[]{:S(2)}) copy-start(bf16[24]{0:T(256)(128)(2,1)} %param.31) | copy-start | bytes 148
  9.4 132.1 %copy-start.28 = (bf16[24]{0:T(256)(128)(2,1)S(1)}, bf16[24]{0:T(256)(128)(2,1)}, u32[]{:S(2)}) copy-start(bf16[24]{0:T(256)(128)(2,1)} %param.30) | copy-start | bytes 148
  9.5 132.4 %copy-start.29 = (bf16[24]{0:T(256)(128)(2,1)S(1)}, bf16[24]{0:T(256)(128)(2,1)}, u32[]{:S(2)}) copy-start(bf16[24]{0:T(256)(128)(2,1)} %param.35) | copy-start | bytes 148
  9.5 132.6 %copy-start.30 = (bf16[16]{0:T(256)(128)(2,1)S(1)}, bf16[16]{0:T(256)(128)(2,1)}, u32[]{:S(2)}) copy-start(bf16[16]{0:T(256)(128)(2,1)} %param.38) | copy-start | bytes 100
  9.5 132.8 %copy-start.31 = (bf16[16]{0:T(256)(128)(2,1)S(1)}, bf16[16]{0:T(256)(128)(2,1)}, u32[]{:S(2)}) copy-start(bf16[16]{0:T(256)(128)(2,1)} %param.37) | copy-start | bytes 100
  9.5 133.1 %copy-start.32 = (bf16[96]{0:T(256)(128)(2,1)S(1)}, bf16[96]{0:T(256)(128)(2,1)}, u32[]{:S(2)}) copy-start(bf16[96]{0:T(256)(128)(2,1)} %param.33) | copy-start | bytes 580
  9.5 256.9 %all-to-all-start.1 = ((bf16[64,32,512]{2,1,0:T(8,128)(2,1)}), bf16[64,32,512]{2,1,0:T(8,128)(2,1)}, u32[]{:S(2)}, u32[]{:S(2)}) async-start(bf16[64,32,512]{2,1,0:T(8,128)(2,1)} %param.39), calls=%async_computation.1 | async-start | bytes 4194304 | tf_op jit(solution)/shard_map/all_to_all | solution.py:249
  17.0 163.8 %copy-start.12 = (bf16[2,256,768]{2,1,0:T(8,128)(2,1)S(1)}, bf16[2,256,768]{2,1,0:T(8,128)(2,1)}, u32[]{:S(2)}) copy-start(bf16[2,256,768]{2,1,0:T(8,128)(2,1)} %param.22) | copy-start | bytes 2359300
  17.0 321.2 %all-gather.12.cloned.1.call-start = ((), (), s32[]{:S(2)}) async-start(), calls=%async_computation.10 | async-start | bytes 4866048 | tf_op jit(solution)/shard_map/all_gather | solution.py:194
  17.6 543.3 %all-reduce.21.cloned.1.call-start = ((), (), s32[]{:S(2)}) async-start(), calls=%async_computation.16 | async-start | bytes 786432
  180.8 0.7 copy-start.20
  181.4 1.4 copy-start.19
  281.4 67.3 %copy-start = (f32[512,768]{1,0:T(8,128)}, f32[512,768]{1,0:T(8,128)S(1)}, u32[]{:S(2)}) copy-start(f32[512,768]{1,0:T(8,128)S(1)} %fusion.18) | copy-start | bytes 4718596
  328.3 1.1 copy-start.2
  338.1 7.5 copy-start.3
  338.1 7.5 copy-start.23
  345.6 3.1 copy-start.33
  348.7 1.3 copy-start.14
  349.4 2.4 copy-start.5
  402.6 1.1 copy-start.15
  403.8 1.1 copy-start.16
  405.7 2.0 copy-start.24
  407.7 2.5 copy-start.10
  407.7 2.6 copy-start.6
  410.8 1.1 copy-start.9
  411.9 1.7 copy-start.4
  413.4 234.7 %reduce-scatter.14.cloned.1.call-start = ((), (), s32[]{:S(2)}) async-start(), calls=%async_computation.15 | async-start | bytes 1622016 | tf_op jit(solution)/shard_map/reduce_scatter | solution.py:348
  413.6 6.9 copy-start.7
  419.6 0.9 copy-start.17
  422.3 330.3 %reduce-scatter.8.cloned.1.call-start = ((), (), s32[]{:S(2)}) async-start(), calls=%async_computation.12 | async-start | bytes 2433024 | tf_op jit(solution)/shard_map/reduce_scatter | solution.py:341
  425.6 1.1 copy-start.11
  425.7 451.8 %reduce-scatter.6.cloned.1.call-start = ((), (), s32[]{:S(2)}) async-start(), calls=%async_computation.11 | async-start | bytes 7299072 | tf_op jit(solution)/shard_map/reduce_scatter | solution.py:340
  433.4 585.7 %reduce-scatter.10.cloned.1.call-start = ((), (), s32[]{:S(2)}) async-start(), calls=%async_computation.13 | async-start | bytes 9732096 | tf_op jit(solution)/shard_map/reduce_scatter | solution.py:344
  440.7 1.4 copy-start.1
  440.7 719.9 %reduce-scatter.12.cloned.1.call-start = ((), (), s32[]{:S(2)}) async-start(), calls=%async_computation.14 | async-start | bytes 9732096 | tf_op jit(solution)/shard_map/reduce_scatter | solution.py:346
  450.3 1.1 copy-start.13
  450.3 1.4 copy-start.18
  482.6 2.9 copy-start.8
  482.6 79.6 %all-to-all-start = ((bf16[2,1024,512]{2,0,1:T(2,128)(2,1)}), bf16[2,1024,512]{2,0,1:T(2,128)(2,1)S(1)}, u32[]{:S(2)}, u32[]{:S(2)}) async-start(bf16[2,1024,512]{2,0,1:T(2,128)(2,1)} %copy.125), calls=%async_computation | async-start | bytes 4194304 | tf_op jit(solution)/shard_map/all_to_all | solution.py:248
Sparse Core Ops, SparseCore 0:
  10.8 73.5 all-gather.5
  87.2 52.7 all-gather.7
  142.8 64.1 all-gather.9
  209.7 63.5 all-gather.11
  413.5 131.6 all-reduce.20
  550.8 97.1 reduce-scatter.13
  653.9 98.6 reduce-scatter.7
  758.9 118.5 reduce-scatter.5
  883.9 135.0 reduce-scatter.9
  1025.4 135.1 reduce-scatter.11
where the time goes:
time: 1170 us
  waiting for transfers between devices  599 us (51%)
  blocking collectives  313 us (27%)
  local copies, waits for them, and re-layouts  133 us (11%)
  matrix products  80.3 us (7%)
  between operations  15.1 us (1%)
    reduce_scatter x1, waiting for transfers between devices, local(): lax.psum_scatter(local_grads[7], ('dp', 'fsdp'), scatter_dimension=0, til...  142 us
    reduce_scatter x1, waiting for transfers between devices, local(): lax.psum_scatter(local_grads[9], ('dp', 'fsdp'), scatter_dimension=0, til...  142 us
    reduce_scatter x1, waiting for transfers between devices, local(): lax.psum_scatter(local_grads[3], ('dp', 'fsdp'), scatter_dimension=0, til...  125 us
    all_gather x1, blocking collectives, local(): lax.all_gather(shards[0], ('dp', 'fsdp'), axis=0, tiled=True)  123 us
    unnamed x2, blocking collectives  106 us
    reduce_scatter x1, waiting for transfers between devices, local(): lax.psum_scatter(local_grads[4], ('dp', 'fsdp'), scatter_dimension=0, til...  105 us
    reduce_scatter x1, waiting for transfers between devices, local(): lax.psum_scatter(local_grads[11], ('dp', 'fsdp'), scatter_dimension=0, ti...  84 us
    all_gather x1, blocking collectives, local(): lax.all_gather(shards[11], ('dp', 'fsdp'), axis=0, tiled=True)  83.6 us
  transfers between devices with their start and end apart: 12, of which 5 were waited for; matrix products, arithmetic and copies ran while one was open for 12% of the time, Pallas kernels for 0%

commit v1 on v0

--- a/solution.py
+++ b/solution.py
@@ -181,6 +181,20 @@
         dec_bias,
         mask_token,
     )
+
+    def wait_the_clusters(at_axis, frame, row_axis):
+        heard, parts_out = (lax.axis_size(row_axis), lax.axis_index(row_axis))
+        left_arr, x_next = (frame, 1)
+        while x_next < heard:
+            block_now = lax.ppermute(
+                left_arr, axis_name=row_axis, perm=[(t, t ^ x_next) for t in range(heard)]
+            )
+            value_now = jnp.concatenate([left_arr, block_now], at_axis)
+            now = jnp.concatenate([block_now, left_arr], axis=at_axis)
+            left_arr = jnp.where(parts_out & x_next == 0, value_now, now)
+            x_next = 2 * x_next
+        return left_arr
+
     gathered = (
         lax.all_gather(shards[0], ("dp", "fsdp"), axis=0, tiled=True),
         lax.all_gather(shards[1], ("dp", "fsdp"), axis=0, tiled=True),
@@ -193,7 +207,7 @@
         lax.all_gather(shards[8], ("dp", "fsdp"), axis=0, tiled=True),
         lax.all_gather(shards[9], ("dp", "fsdp"), axis=0, tiled=True),
         lax.all_gather(shards[10], ("dp", "fsdp"), axis=0, tiled=True),
-        lax.all_gather(shards[11], ("dp", "fsdp"), axis=0, tiled=True),
+        wait_the_clusters(0, shards[11], ("dp", "fsdp")),
         lax.all_gather(shards[12], ("dp", "fsdp"), axis=0, tiled=True),
         lax.all_gather(shards[13], ("dp", "fsdp"), axis=0, tiled=True),
     )

time: 1170 us -> 1180 us (level)
    ppermute x0 -> x5, waiting for transfers between devices: none -> 25.8 us  [wait_the_clusters(): lax.ppermute(left_arr, axis_name=row_axis, perm=[(t, t ^ x_next) for t in...]
    reduce_scatter x1, waiting for transfers between devices: 84 us -> 61.9 us  [local(): lax.psum_scatter(local_grads[11], ('dp', 'fsdp'), scatter_dimension=0, ti...]
  transfers between devices with their start and end apart: 12 -> 17, of which waited for: 5 -> 10; matrix products, arithmetic and copies ran while one was open for 12% -> 12% of each run, Pallas kernels for 0% -> 0%
where the time goes in v1:
time: 1180 us; the launch traced here: 1170 us
  waiting for transfers between devices  603 us (51%)
  blocking collectives  313 us (27%)
  local copies, waits for them, and re-layouts  132 us (11%)
  matrix products  80.5 us (7%)
  between operations  15.2 us (1%)
  starting transfers between devices  13.3 us (1%)
    reduce_scatter x1, waiting for transfers between devices, local(): lax.psum_scatter(local_grads[7], ('dp', 'fsdp'), scatter_dimension=0, til...  142 us
    reduce_scatter x1, waiting for transfers between devices, local(): lax.psum_scatter(local_grads[9], ('dp', 'fsdp'), scatter_dimension=0, til...  141 us
    reduce_scatter x1, waiting for transfers between devices, local(): lax.psum_scatter(local_grads[3], ('dp', 'fsdp'), scatter_dimension=0, til...  125 us
    all_gather x1, blocking collectives, local(): lax.all_gather(shards[0], ('dp', 'fsdp'), axis=0, tiled=True)  123 us
    unnamed x2, blocking collectives  106 us
    reduce_scatter x1, waiting for transfers between devices, local(): lax.psum_scatter(local_grads[4], ('dp', 'fsdp'), scatter_dimension=0, til...  105 us
    all_gather x1, blocking collectives, local(): lax.all_gather(shards[11], ('dp', 'fsdp'), axis=0, tiled=True)  83.8 us
    reduce_scatter x1, waiting for transfers between devices, local(): lax.psum_scatter(local_grads[11], ('dp', 'fsdp'), scatter_dimension=0, ti...  61.9 us
  transfers between devices with their start and end apart: 17, of which 10 were waited for; matrix products, arithmetic and copies ran while one was open for 12% of the time, Pallas kernels for 0%

profile of v1, /device:TPU:0, one launch (start us, length us, event | category | flops | bytes accessed | tf_op | source)
XLA Modules:
  0.0 1173.1 jit_solution(10549479731364341745)
XLA Ops:
  9.5 7.5 all-to-all-start.1
  17.7 123.0 %all-gather = bf16[32,4,768]{2,1,0:T(4,128)(2,1)S(1)} all-gather(bf16[1,4,768]{2,1,0:T(4,128)(2,1)S(1)} %bitcast.242), channel_id=1, replica_groups=mesh['dp'=8,'fsdp'=4] {'dp','fsdp'}, dimensions={0}, use_global_device_ids=true | all-gather | bytes 202752 | tf_op jit(solution)/shard_map/all_gather | solution.py:199
  142.8 37.7 %all-reduce.18 = (bf16[512]{0:T(512)(128)(2,1)S(1)}, bf16[768]{0:T(1024)(128)(2,1)S(1)}, bf16[768]{0:T(1024)(128)(2,1)S(1)}, bf16[768]{0:T(1024)(128)(2,1)S(1)},...) all-reduce(bf16[512]{0:T(512)(128)(2,1)S(1)} %dynamic-update-slice,, ...), channel_id=1, replica_groups=mesh['dp'=8,'fsdp'=4] {'dp','fsdp'}, use_global_device_ids=true, to_apply=%add | all-reduce | flops 7936 | bytes 31744
  181.5 1.2 add_convert_fusion.2
  182.8 83.8 %all_gather.61 = bf16[768,512]{1,0:T(8,128)(2,1)} all-gather(bf16[24,512]{1,0:T(8,128)(2,1)S(1)} %copy-done.18), channel_id=1, replica_groups=mesh['dp'=8,'fsdp'=4] {'dp','fsdp'}, dimensions={0}, use_global_device_ids=true | all-gather | bytes 811008 | tf_op jit(solution)/shard_map/all_gather | solution.py:276
  266.6 3.2 copy.128
  269.7 9.9 gather_fusion
  279.7 1.9 fusion.24
  281.6 4.8 convolution_convert_fusion.1
  286.4 1.5 fusion.42
  287.9 2.3 copy.121
  290.2 2.3 copy.122
  292.5 2.3 copy.123
  294.8 28.2 %while.30 = (s32[]{:T(128)}, bf16[6,2,256,128]{2,3,1,0:T(8,128)(2,1)}, f32[6,2,2,256,1]{3,2,1,4,0:T(2,128)S(1)}, s32[6]{0:T(128)S(1)}, bf16[2,256,768]{1,2,0:T(8...) while((s32[]{:T(128)}, ...), condition=%wide.region_6.7_spmd, body=%wide.region_3.6_spmd.sunk | while | flops 69008384 | bytes 4751551 | solution.py:91
  296.0 0.9 constant_dynamic-slice_fusion.14
  297.0 1.0 constant_dynamic-slice_fusion.15
  300.8 0.9 constant_dynamic-slice_fusion.14
  301.7 1.0 constant_dynamic-slice_fusion.15
  305.5 0.9 constant_dynamic-slice_fusion.14
  306.4 1.0 constant_dynamic-slice_fusion.15
  310.2 0.9 constant_dynamic-slice_fusion.14
  311.1 1.0 constant_dynamic-slice_fusion.15
  315.8 1.0 constant_dynamic-slice_fusion.15
  320.5 1.0 constant_dynamic-slice_fusion.15
  323.1 1.9 copy.124
  325.0 1.1 copy.144
  326.1 2.4 fusion.43
  328.5 1.1 copy-done.2
  330.0 8.4 multiply_convert_fusion.1
  338.4 7.5 convert_reduce_fusion
  345.9 3.1 multiply_reduce_fusion.1
  350.2 1.8 convolution_convert_fusion.2
  352.1 49.0 %while.31 = (s32[]{:T(128)}, bf16[6,2,256,128]{2,3,1,0:T(8,128)(2,1)}, bf16[6,2,256,128]{2,3,1,0:T(8,128)(2,1)}, bf16[6,2,256,128]{2,3,1,0:T(8,128)(2,1)}, s32[6...) while((s32[]{:T(128)}, ...), condition=%wide.region_14.15_spmd, body=%wide.region_12.14_spmd.sunk | while | flops 170130432 | bytes 11292899 | solution.py:137
  401.1 1.9 copy.133
  406.4 1.7 copy-done.23
  408.1 2.5 multiply_reduce_fusion.2
  411.2 1.1 copy-done.9
  412.5 1.3 fusion.44
  414.0 6.0 add_convert_fusion
  420.9 1.8 fusion.23
  422.8 3.3 fusion.20
  426.2 1.1 copy-done.11
  427.2 6.6 fusion.45
  433.9 7.2 fusion.39
  441.5 1.1 copy-done.1
  442.6 8.2 fusion.33
  450.9 3.8 collective-permute-done
  454.8 5.0 collective-permute-done.1
  459.9 1.3 collective-permute-done.2
  461.3 7.0 collective-permute-done.3
  468.5 1.8 collective-permute-start.4
  470.3 8.6 collective-permute-done.4
  479.7 26.7 %scatter_fusion = bf16[2,1024,512]{2,1,0:T(8,128)(2,1)S(1)} fusion(bf16[2,1024,512]{2,1,0:T(8,128)(2,1)S(1)} %broadcast_in_dim.84, s32[512]{0:T(512)S(1)} %bitcast.199, bf16[512,512]{1,0:T(8,128)(2,1)S(1)} %fusion.12), kind=kCustom, calls=%fused_computation.1 | custom fusion | bytes 1576960 | tf_op jit(solution)/shard_map/scatter | solution.py:261
  506.5 3.5 copy.125
  509.9 2.9 all-to-all-start
  513.0 1.9 convert_reduce_fusion.1
  515.0 68.7 %all-reduce.17 = (f32[768]{0:T(1024)S(1)}, f32[768]{0:T(1024)S(1)}, f32[768]{0:T(1024)S(1)}, f32[768]{0:T(1024)S(1)}, f32[3072]{0:T(1024)S(1)}, /*index=5*/f32[768]{0:T(1024)S(1)}, f32[512]{0:T(512)S(1)}, f32[512]{0:T(512)S(1)}) all-reduce(f32[768]{0:T(1024)S(1)} %get-tuple-element.342, ...), channel_id=3, replica_groups=mesh['dp'=8,'fsdp'=4] {'dp','fsdp'}, use_global_device_ids=true, to_apply=%region_20.21.clone | all-reduce | flops 7936 | bytes 63488
  588.3 1.3 constant_dynamic-slice_fusion.7
  590.0 1.6 copy.127
  591.6 61.9 %reduce-scatter.14.cloned.1.call-done = f32[24,512]{1,0:T(8,128)} async-done(((f32[768,512]{1,0:T(8,128)}), f32[24,512]{1,0:T(8,128)}) %reduce-scatter.14.cloned.1.call-update) | async-done | bytes 49168 | tf_op jit(solution)/shard_map/reduce_scatter | solution.py:362
  653.5 104.5 %reduce-scatter.8.cloned.1.call-done = f32[24,768]{1,0:T(8,128)} async-done(((f32[768,768]{1,0:T(8,128)}), f32[24,768]{1,0:T(8,128)}) %reduce-scatter.8.cloned.1.call-update) | async-done | bytes 73744 | tf_op jit(solution)/shard_map/reduce_scatter | solution.py:355
  758.1 124.8 %reduce-scatter.6.cloned.1.call-done = f32[24,2304]{1,0:T(8,128)} async-done(((f32[768,2304]{1,0:T(8,128)}), f32[24,2304]{1,0:T(8,128)}) %reduce-scatter.6.cloned.1.call-update) | async-done | bytes 221200 | tf_op jit(solution)/shard_map/reduce_scatter | solution.py:354
  882.9 141.6 %reduce-scatter.10.cloned.1.call-done = f32[24,3072]{1,0:T(8,128)} async-done(((f32[768,3072]{1,0:T(8,128)}), f32[24,3072]{1,0:T(8,128)}) %reduce-scatter.10.cloned.1.call-update) | async-done | bytes 294928 | tf_op jit(solution)/shard_map/reduce_scatter | solution.py:358
  1024.5 141.4 %reduce-scatter.12.cloned.1.call-done = f32[96,768]{1,0:T(8,128)} async-done(((f32[3072,768]{1,0:T(8,128)}), f32[96,768]{1,0:T(8,128)}) %reduce-scatter.12.cloned.1.call-update) | async-done | bytes 294928 | tf_op jit(solution)/shard_map/reduce_scatter | solution.py:360
  (299 shorter events, 78.7 us)
Async XLA Ops:
  7.2 274.4 %all-gather.6.cloned.1.call-start = ((), (), s32[]{:S(2)}) async-start(), calls=%async_computation.7 | async-start | bytes 3649536 | tf_op jit(solution)/shard_map/all_gather | solution.py:202
  7.9 318.2 %all-gather.8.cloned.1.call-start = ((), (), s32[]{:S(2)}) async-start(), calls=%async_computation.8 | async-start | bytes 1216512 | tf_op jit(solution)/shard_map/all_gather | solution.py:203
  8.7 321.3 %all-gather.10.cloned.1.call-start = ((), (), s32[]{:S(2)}) async-start(), calls=%async_computation.9 | async-start | bytes 4866048 | tf_op jit(solution)/shard_map/all_gather | solution.py:206
  9.4 8.3 copy-start.20
  9.4 131.4 %copy-start.21 = (s32[2,13]{1,0:T(2,128)S(1)}, s32[2,13]{1,0:T(2,128)}, u32[]{:S(2)}) copy-start(s32[2,13]{1,0:T(2,128)} %param.23) | copy-start | bytes 316
  9.4 131.5 %copy-start.24 = (bf16[24]{0:T(256)(128)(2,1)S(1)}, bf16[24]{0:T(256)(128)(2,1)}, u32[]{:S(2)}) copy-start(bf16[24]{0:T(256)(128)(2,1)} %param.27) | copy-start | bytes 148
  9.4 131.7 %copy-start.25 = (bf16[24]{0:T(256)(128)(2,1)S(1)}, bf16[24]{0:T(256)(128)(2,1)}, u32[]{:S(2)}) copy-start(bf16[24]{0:T(256)(128)(2,1)} %param.26) | copy-start | bytes 148
  9.4 131.9 %copy-start.26 = (bf16[24]{0:T(256)(128)(2,1)S(1)}, bf16[24]{0:T(256)(128)(2,1)}, u32[]{:S(2)}) copy-start(bf16[24]{0:T(256)(128)(2,1)} %param.31) | copy-start | bytes 148
  9.4 132.1 %copy-start.27 = (bf16[24]{0:T(256)(128)(2,1)S(1)}, bf16[24]{0:T(256)(128)(2,1)}, u32[]{:S(2)}) copy-start(bf16[24]{0:T(256)(128)(2,1)} %param.30) | copy-start | bytes 148
  9.5 132.4 %copy-start.28 = (bf16[24]{0:T(256)(128)(2,1)S(1)}, bf16[24]{0:T(256)(128)(2,1)}, u32[]{:S(2)}) copy-start(bf16[24]{0:T(256)(128)(2,1)} %param.35) | copy-start | bytes 148
  9.5 132.6 %copy-start.29 = (bf16[16]{0:T(256)(128)(2,1)S(1)}, bf16[16]{0:T(256)(128)(2,1)}, u32[]{:S(2)}) copy-start(bf16[16]{0:T(256)(128)(2,1)} %param.38) | copy-start | bytes 100
  9.5 132.8 %copy-start.30 = (bf16[16]{0:T(256)(128)(2,1)S(1)}, bf16[16]{0:T(256)(128)(2,1)}, u32[]{:S(2)}) copy-start(bf16[16]{0:T(256)(128)(2,1)} %param.37) | copy-start | bytes 100
  9.5 133.1 %copy-start.31 = (bf16[96]{0:T(256)(128)(2,1)S(1)}, bf16[96]{0:T(256)(128)(2,1)}, u32[]{:S(2)}) copy-start(bf16[96]{0:T(256)(128)(2,1)} %param.33) | copy-start | bytes 580
  9.5 257.1 %all-to-all-start.1 = ((bf16[64,32,512]{2,1,0:T(8,128)(2,1)}), bf16[64,32,512]{2,1,0:T(8,128)(2,1)}, u32[]{:S(2)}, u32[]{:S(2)}) async-start(bf16[64,32,512]{2,1,0:T(8,128)(2,1)} %param.39), calls=%async_computation.1 | async-start | bytes 4194304 | tf_op jit(solution)/shard_map/all_to_all | solution.py:263
  17.0 163.8 %copy-start.12 = (bf16[2,256,768]{2,1,0:T(8,128)(2,1)S(1)}, bf16[2,256,768]{2,1,0:T(8,128)(2,1)}, u32[]{:S(2)}) copy-start(bf16[2,256,768]{2,1,0:T(8,128)(2,1)} %param.22) | copy-start | bytes 2359300
  17.0 321.4 %all-gather.12.cloned.1.call-start = ((), (), s32[]{:S(2)}) async-start(), calls=%async_computation.10 | async-start | bytes 4866048 | tf_op jit(solution)/shard_map/all_gather | solution.py:208
  17.6 570.8 %all-reduce.21.cloned.1.call-start = ((), (), s32[]{:S(2)}) async-start(), calls=%async_computation.16 | async-start | bytes 786432
  180.8 0.7 copy-start.19
  181.4 1.4 copy-start.18
  281.6 67.4 %copy-start = (f32[512,768]{1,0:T(8,128)}, f32[512,768]{1,0:T(8,128)S(1)}, u32[]{:S(2)}) copy-start(f32[512,768]{1,0:T(8,128)S(1)} %fusion.24) | copy-start | bytes 4718596
  328.5 1.1 copy-start.2
  338.4 7.5 copy-start.3
  338.4 7.5 copy-start.22
  345.8 3.1 copy-start.32
  349.0 1.3 copy-start.13
  349.6 2.5 copy-start.5
  403.0 1.1 copy-start.14
  404.2 1.1 copy-start.15
  406.1 2.0 copy-start.23
  408.1 2.5 copy-start.10
  408.1 2.6 copy-start.6
  411.2 1.1 copy-start.9
  412.4 1.7 copy-start.4
  413.8 239.8 %reduce-scatter.14.cloned.1.call-start = ((), (), s32[]{:S(2)}) async-start(), calls=%async_computation.15 | async-start | bytes 1622016 | tf_op jit(solution)/shard_map/reduce_scatter | solution.py:362
  414.0 6.9 copy-start.7
  420.0 0.9 copy-start.16
  422.7 335.3 %reduce-scatter.8.cloned.1.call-start = ((), (), s32[]{:S(2)}) async-start(), calls=%async_computation.12 | async-start | bytes 2433024 | tf_op jit(solution)/shard_map/reduce_scatter | solution.py:355
  426.1 1.1 copy-start.11
  426.1 456.8 %reduce-scatter.6.cloned.1.call-start = ((), (), s32[]{:S(2)}) async-start(), calls=%async_computation.11 | async-start | bytes 7299072 | tf_op jit(solution)/shard_map/reduce_scatter | solution.py:354
  433.9 590.6 %reduce-scatter.10.cloned.1.call-start = ((), (), s32[]{:S(2)}) async-start(), calls=%async_computation.13 | async-start | bytes 9732096 | tf_op jit(solution)/shard_map/reduce_scatter | solution.py:358
  441.2 1.4 copy-start.1
  441.2 724.8 %reduce-scatter.12.cloned.1.call-start = ((), (), s32[]{:S(2)}) async-start(), calls=%async_computation.14 | async-start | bytes 9732096 | tf_op jit(solution)/shard_map/reduce_scatter | solution.py:360
  450.8 28.2 %copy-start.17 = (bf16[512,768]{1,0:T(8,128)(2,1)S(1)}, bf16[512,768]{1,0:T(8,128)(2,1)}, u32[]{:S(2)}) copy-start(bf16[512,768]{1,0:T(8,128)(2,1)} %copy-done.16) | copy-start | bytes 2359300
  450.8 3.9 collective-permute-start
  454.7 5.1 collective-permute-start.1
  459.8 1.4 collective-permute-start.2
  461.2 7.1 collective-permute-start.3
  468.5 10.5 collective-permute-start.4
  509.9 2.9 copy-start.8
  509.9 79.8 %all-to-all-start = ((bf16[2,1024,512]{2,0,1:T(2,128)(2,1)}), bf16[2,1024,512]{2,0,1:T(2,128)(2,1)S(1)}, u32[]{:S(2)}, u32[]{:S(2)}) async-start(bf16[2,1024,512]{2,0,1:T(2,128)(2,1)} %copy.125), calls=%async_computation | async-start | bytes 4194304 | tf_op jit(solution)/shard_map/all_to_all | solution.py:262
Sparse Core Ops, SparseCore 0:
  10.8 73.5 all-gather.5
  87.2 52.7 all-gather.7
  142.8 64.1 all-gather.9
  209.7 63.4 all-gather.11
  413.9 136.1 all-reduce.20
  555.8 97.7 reduce-scatter.13
  659.4 98.6 reduce-scatter.7
  764.3 118.5 reduce-scatter.5
  889.4 135.0 reduce-scatter.9
  1030.8 135.0 reduce-scatter.11
